TPU v7x, 256 devices: a whole 4x4x8 slice. The times are simulated.
256 devices in a mesh: ka: 16 (over z, y_lo), band: 8 (over x, y_hi), ga: 2 (over core).
Axes of the slice: x: 4, y: 4 (y_hi: 2, y_lo: 2; y = y_hi * 2 + y_lo), z: 8, core: 2. Of those that a mesh axis runs over, the one named last changes fastest.
Arguments:
- pair_density: bfloat16 [8, 256, 8, 2048], P(None, ('ka', 'band')), may hold values from -4 to 4
- valence_energy: float32 [8, 8], replicated, may hold values from -6 to -1
- conduction_energy: float32 [8, 256], replicated, may hold values from 0.5 to 12
- star_map: int32 [64], replicated, may hold values from 0 to 7, as said below
- op_of_k: int32 [64], replicated, may hold values from 0 to 47
- perm_lists: int32 [48, 2048], replicated, may hold values from 0 to 2047, as said below
- cond_top: int32 [64], replicated, may hold values from 128 to 256
Outputs:
- chi: float32 [1, 2048, 2048], P(None, ('band', 'ga'), 'ka')
Inputs may be any that keep to these rules, and one draw needn't show every extreme that they name: `star_map`: every irreducible point is named by at least one full-zone k-point. `perm_lists`: each row is a permutation of 0 .. 2047 that maps every aligned block of 128 slots onto itself.
All inputs are finite; a program needn't handle non-finite values.
Results may differ from a plain program's by a relative error of at most 0.0015.
Values may be sent and summed in bfloat16 or wider, within the bound.
No kernel may reach another device: no remote copies, remote signals or barrier semaphores. Data moves between devices by JAX's collectives and lax.ppermute only.
A program may use at most 128 MiB of HBM per device.

v0:
```python
import jax
import jax.numpy as jnp
from jax import lax
from jax.sharding import PartitionSpec as P

NG = 2048
GB = 128
KI = 8
KF = 64
NF = 1
freq_step = 2.0


def rotate_batch(picked, perm_rows):
    k_count = picked.shape[0]
    blocks = NG // GB
    local = perm_rows.reshape(k_count, blocks, GB) - (jnp.arange(blocks) * GB)[None, :, None]
    onehot = (local[..., None] == jnp.arange(GB)[None, None, None, :]).astype(jnp.bfloat16)
    shaped = picked.reshape(k_count, -1, blocks, GB)
    moved = jnp.einsum("krbi,kboi->krbo", shaped, onehot, preferred_element_type=jnp.float32)
    return moved.astype(jnp.bfloat16).reshape(picked.shape)


def on_device(
    pair_density, valence_energy, conduction_energy, star_map, op_of_k, perm_lists, cond_top
):
    ka_count = lax.axis_size("ka")
    band_count = lax.axis_size("band")
    ga_count = lax.axis_size("ga")
    ka_index = lax.axis_index("ka")
    band_index = lax.axis_index("band")
    ga_index = lax.axis_index("ga")
    k_local = KF // ka_count
    cond_piece = pair_density.shape[1]
    my_points = ka_index * k_local + jnp.arange(k_local)
    stars = jnp.take(star_map, my_points)
    tops = jnp.take(cond_top, my_points)
    whole = lax.all_gather(pair_density, "ka", axis=1, tiled=True)
    picked = jnp.take(whole, stars, axis=0)
    my_perms = jnp.take(perm_lists, jnp.take(op_of_k, my_points), axis=0)
    rotated = rotate_batch(picked, my_perms)
    cond_table = conduction_energy.reshape(KI, ka_count, band_count, cond_piece)
    cond_table = lax.dynamic_slice_in_dim(cond_table, band_index, 1, 2).reshape(
        KI, ka_count * cond_piece
    )
    cond_local = jnp.take(cond_table, stars, axis=0)
    val_local = jnp.take(valence_energy, stars, axis=0)
    band_global = (
        jnp.arange(ka_count)[:, None] * band_count + band_index
    ) * cond_piece + jnp.arange(cond_piece)[None, :]
    band_global = band_global.reshape(ka_count * cond_piece)
    mask = (band_global[None, :] < tops[:, None]).astype(jnp.float32)[None, :, :, None]
    omega = freq_step * jnp.arange(NF).astype(jnp.float32)
    omega_sq = (omega * omega)[:, None, None, None]
    diff = val_local[:, None, :] - cond_local[:, :, None]
    weight = 4.0 / KF * diff[None] / (diff[None] * diff[None] + omega_sq) * mask
    product = weight[..., None] * rotated[None].astype(jnp.float32)
    scaled_hi = product.astype(jnp.bfloat16)
    hi_back = lax.optimization_barrier(scaled_hi).astype(jnp.float32)
    scaled_lo = (product - hi_back).astype(jnp.bfloat16)
    pair_rows = rotated.shape[0] * rotated.shape[1] * rotated.shape[2]
    flat_scaled = jnp.stack(
        [scaled_hi.reshape(NF, pair_rows, NG), scaled_lo.reshape(NF, pair_rows, NG)]
    )
    flat = rotated.reshape(pair_rows, NG)
    slab = NG // (band_count * ga_count)
    row_part = flat.reshape(pair_rows, band_count, ga_count, slab)
    row_part = lax.dynamic_slice_in_dim(row_part, ga_index, 1, 2).reshape(
        pair_rows, band_count * slab
    )
    partial_value = jnp.einsum(
        "rg,sfrh->fgh", row_part, flat_scaled, preferred_element_type=jnp.float32
    )
    column_sums = lax.psum_scatter(partial_value, "ka", scatter_dimension=2, tiled=True)
    return lax.psum_scatter(column_sums, "band", scatter_dimension=1, tiled=True)


def solution(mesh):
    return jax.shard_map(
        on_device,
        mesh=mesh,
        in_specs=(P(None, ("ka", "band"), None, None), P(), P(), P(), P(), P(), P()),
        out_specs=P(None, ("band", "ga"), "ka"),
        check_vma=False,
    )
```

profile of v0, /device:TPU:2, one launch (start us, length us, event | category | flops | bytes accessed | tf_op | source)
XLA Modules:
  0.0 547.9 jit_solution(13602813167420612139)
XLA Ops:
  6.5 0.0 copy-start
  6.5 0.0 all-gather.2.cloned.1.call-start
  6.5 0.7 all-gather.2.cloned.1.call-update
  7.3 0.0 reduce-scatter.3.cloned.1.call-start
  7.3 1.3 gather_fusion.6
  8.6 1.3 gather_fusion.5
  9.9 1.3 gather_fusion.4
  11.2 0.1 iota_add_fusion
  11.3 0.1 add.71
  11.4 0.8 copy.11
  12.3 0.1 copy.12
  12.3 1.2 gather_fusion
  13.6 0.6 gather_fusion.1
  14.2 0.1 compare_convert_fusion
  14.2 0.1 broadcast_select_fusion.1
  14.3 0.1 broadcast_select_fusion
  14.4 0.1 fusion.6
  14.5 0.1 mul.115
  14.6 0.0 copy-done
  14.6 0.6 gather_fusion.2
  15.2 0.1 fusion.7
  15.3 179.3 %all-gather.2.cloned.1.call-done = bf16[8,32,8,2048]{3,2,1,0:T(8,128)(2,1)} async-done(((bf16[8,2,8,2048]{3,2,1,0:T(8,128)(2,1)}), bf16[8,32,8,2048]{3,2,1,0:T(8,128)(2,1)}) %all-gather.2.cloned.1.call-update) | async-done | bytes 8388624 | tf_op jit(solution)/shard_map/all_gather | solution.py:38
  194.5 6.2 %gather_fusion.3 = bf16[4,32,8,2048]{3,2,1,0:T(8,128)(2,1)} fusion(bf16[8,32,8,2048]{3,2,1,0:T(8,128)(2,1)} %all-gather.2.cloned.1.call-done, s32[1024]{0:T(1024)S(1)} %pad_clamp_fusion.1), kind=kCustom, calls=%fused_computation.6 | custom fusion | bytes 8388624 | tf_op jit(solution)/shard_map/jit(_take)/gather | solution.py:39
  200.7 3.6 copy.20
  204.3 3.7 convert_bitcast_fusion
  208.0 6.4 %copy.16 = bf16[4,256,16,128]{3,1,0,2:T(8,128)(2,1)} copy(bf16[4,256,16,128]{1,3,2,0:T(8,128)(2,1)} %convert_bitcast_fusion) | data formatting | bytes 8388608 | tf_op jit(solution)/shard_map/convert_element_type | solution.py:21
  214.4 8.4 %copy.14 = f32[4,256,16,128]{3,2,1,0:T(8,128)} copy(bf16[4,256,16,128]{1,3,2,0:T(8,128)(2,1)} %convert_bitcast_fusion) | data formatting | bytes 12582912 | tf_op jit(solution)/shard_map/convert_element_type | solution.py:57
  222.7 9.3 %reshape.255 = f32[1,4,32,8,2048]{4,3,2,1,0:T(8,128)} reshape(f32[4,256,16,128]{3,2,1,0:T(8,128)} %copy.14) | data formatting | bytes 16777216 | tf_op jit(solution)/shard_map/convert_element_type | solution.py:57
  232.0 9.2 %reshape.254 = f32[1,1024,2048]{2,1,0:T(8,128)} reshape(f32[4,256,16,128]{3,2,1,0:T(8,128)} %copy.14) | data formatting | bytes 16777216 | tf_op jit(solution)/shard_map/convert_element_type | solution.py:57
  241.3 1.7 constant_dynamic-slice_fusion
  243.0 2.6 copy.17
  245.6 0.0 slice-start
  245.6 4.0 multiply_convert_fusion.1
  249.7 0.0 slice-start.1
  249.7 6.5 %subtract_convert_fusion = bf16[1,4,32,8,2048]{4,3,2,1,0:T(8,128)(2,1)} fusion(bf16[1,4,32,8,2048]{4,3,2,1,0:T(8,128)(2,1)S(1)} %multiply_convert_fusion.1, f32[1,4,32,8,2048]{4,3,2,1,0:T(8,128)} %reshape.255, f32[4,32,8]{2,1,0:T(8,128)S(1)} %fusion.6), kind=kLoop, calls=%fused_computation.8 | loop fusion | flops 8388608 | bytes 16781312 | tf_op jit(solution)/shard_map/convert_element_type | solution.py:60
  256.2 0.0 slice-done
  256.2 0.0 slice-done.1
  256.2 0.5 fusion
  256.7 7.4 %convert_reduce_fusion = bf16[1024,2048]{1,0:T(8,128)(2,1)} fusion(bf16[1,1,1024,2048]{3,2,1,0:T(8,128)(2,1)} %bitcast.31, bf16[1,1,1024,2048]{3,2,1,0:T(8,128)(2,1)S(1)} %fusion), kind=kLoop, calls=%fused_computation.7 | loop fusion | flops 18874368 | bytes 12582912 | tf_op jit(solution)/shard_map/rg,sfrh->fgh/reduce_sum | solution.py:71
  264.1 10.7 %convolution_bitcast_fusion = f32[1,1024,2048]{1,2,0:T(8,128)} fusion(bf16[1024,2048]{1,0:T(8,128)(2,1)} %convert_reduce_fusion, bf16[1024,1024]{0,1:T(8,128)(2,1)} %bitcast.35), kind=kOutput, calls=%fused_computation.11 | convolution fusion | flops 4294967296 | bytes 14680064 | tf_op jit(solution)/shard_map/rg,sfrh->fgh/dot_general | solution.py:71
  274.8 0.0 copy-start.1
  274.8 0.0 reduce-scatter.3.cloned.1.call-update
  274.8 0.0 reduce-scatter.5.cloned.1.call-start
  274.9 183.7 %reduce-scatter.3.cloned.1.call-done = f32[1,1024,128]{1,2,0:T(8,128)} async-done(((f32[1,1024,2048]{1,2,0:T(8,128)}), f32[1,1024,128]{1,2,0:T(8,128)}) %reduce-scatter.3.cloned.1.call-update) | async-done | bytes 524304 | tf_op jit(solution)/shard_map/reduce_scatter | solution.py:74
  458.6 0.0 reduce-scatter.5.cloned.1.call-update
  458.6 81.2 %reduce-scatter.5.cloned.1.call-done = f32[1,128,128]{1,2,0:T(8,128)} async-done(((f32[1,1024,128]{1,2,0:T(8,128)}), f32[1,128,128]{1,2,0:T(8,128)}) %reduce-scatter.5.cloned.1.call-update) | async-done | bytes 65552 | tf_op jit(solution)/shard_map/reduce_scatter | solution.py:75
  539.8 1.6 copy.18
  541.3 0.0 copy-done.1
  (10 shorter events, 0.1 us)
Async XLA Ops:
  6.5 8.1 %copy-start = (s32[48,2048]{1,0:T(8,128)S(1)}, s32[48,2048]{1,0:T(8,128)}, u32[]{:S(2)}) copy-start(s32[48,2048]{1,0:T(8,128)} %param.14) | copy-start | bytes 1179652
  6.5 188.0 %all-gather.2.cloned.1.call-start = ((), (), s32[]{:S(2)}) async-start(), calls=%async_computation.2 | async-start | bytes 8912896 | tf_op jit(solution)/shard_map/all_gather | solution.py:38
  7.3 451.3 %reduce-scatter.3.cloned.1.call-start = ((), (), s32[]{:S(2)}) async-start(), calls=%async_computation.3 | async-start | bytes 8912896 | tf_op jit(solution)/shard_map/reduce_scatter | solution.py:74
  245.6 10.5 %slice-start = ((s8[8388608]{0:T(1024)(128)(4,1)}), s8[4194304]{0:T(1024)(128)(4,1)S(1)}, s32[]{:S(2)}) async-start(s8[8388608]{0:T(1024)(128)(4,1)} %bitcast.29), calls=%async_computation.5 | async-start | bytes 8388608
  249.7 6.5 %slice-start.1 = ((s8[8388608]{0:T(1024)(128)(4,1)}), s8[4194304]{0:T(1024)(128)(4,1)S(1)}, s32[]{:S(2)}) async-start(s8[8388608]{0:T(1024)(128)(4,1)} %bitcast.29), calls=%async_computation.6 | async-start | bytes 8388608
  274.8 266.5 %copy-start.1 = (s32[48,2048]{1,0:T(8,128)S(1)}, s32[48,2048]{1,0:T(8,128)}, u32[]{:S(2)}) copy-start(s32[48,2048]{1,0:T(8,128)} %param.14) | copy-start | bytes 1179652
  274.8 264.9 %reduce-scatter.5.cloned.1.call-start = ((), (), s32[]{:S(2)}) async-start(), calls=%async_computation.4 | async-start | bytes 589824 | tf_op jit(solution)/shard_map/reduce_scatter | solution.py:75
Sparse Core Ops, SparseCore 0:
  9.1 185.3 all-gather.1
  274.9 183.5 reduce-scatter.2
  462.5 77.2 reduce-scatter.4
where the time goes:
time: 549 us; the launch traced here: 548 us
  waiting for transfers between devices  445 us (81%)
  local copies, waits for them, and re-layouts  56.3 us (10%)
  other arithmetic  18.9 us (3%)
  matrix products  14.4 us (3%)
  between operations  13.3 us (2%)
    reduce_scatter x1, waiting for transfers between devices, on_device(): lax.psum_scatter(partial_value, 'ka', scatter_dimension=2, tiled=True)  184 us
    all_gather x1, waiting for transfers between devices, on_device(): whole = lax.all_gather(pair_density, 'ka', axis=1, tiled=True)  179 us
    reduce_scatter x1, waiting for transfers between devices, on_device(): lax.psum_scatter(column_sums, 'band', scatter_dimension=1, tiled=True)  81.2 us
    convert_element_type x3, local copies, waits for them, and re-layouts, on_device(): product = weight[..., None] * rotated[None].astype(jnp.float32)  26.9 us
  transfers between devices with their start and end apart: 3, of which 3 were waited for; matrix products, arithmetic and copies ran while one was open for 1% of the time, Pallas kernels for 0%

commit v1 on v0

--- a/solution.py
+++ b/solution.py
@@ -9,6 +9,13 @@
 KF = 64
 NF = 1
 freq_step = 2.0
+
+
+def all_by_exchange(shard, axis, along):
+    count = lax.axis_size(axis)
+    pieces = jnp.stack([shard for _ in range(count)])
+    pieces = lax.all_to_all(pieces, axis, split_axis=0, concat_axis=0)
+    return jnp.concatenate(pieces, axis=along)
 
 
 def rotate_batch(picked, perm_rows):
@@ -35,7 +42,7 @@
     my_points = ka_index * k_local + jnp.arange(k_local)
     stars = jnp.take(star_map, my_points)
     tops = jnp.take(cond_top, my_points)
-    whole = lax.all_gather(pair_density, "ka", axis=1, tiled=True)
+    whole = all_by_exchange(pair_density, "ka", 1)
     picked = jnp.take(whole, stars, axis=0)
     my_perms = jnp.take(perm_lists, jnp.take(op_of_k, my_points), axis=0)
     rotated = rotate_batch(picked, my_perms)

time: 549 us -> 577 us (1.051)
  local copies, waits for them, and re-layouts: 56.3 us -> 66.6 us
  starting transfers between devices: 0.08 us -> 9.86 us
  waiting for transfers between devices: 445 us -> 452 us
    all_to_all x0 -> x1, waiting for transfers between devices: none -> 187 us  [all_by_exchange(): pieces = lax.all_to_all(pieces, axis, split_axis=0, concat_axis=0)]
    all_gather x1 -> x0, waiting for transfers between devices: 179 us -> none  [on_device(): whole = lax.all_gather(pair_density, 'ka', axis=1, tiled=True)]
    all_to_all x0 -> x1, starting transfers between devices: none -> 9.78 us  [all_by_exchange(): pieces = lax.all_to_all(pieces, axis, split_axis=0, concat_axis=0)]
    all_to_all x0 -> x1, local copies, waits for them, and re-layouts: none -> 8.28 us  [all_by_exchange(): pieces = lax.all_to_all(pieces, axis, split_axis=0, concat_axis=0)]
where the time goes in v1:
time: 577 us; the launch traced here: 576 us
  waiting for transfers between devices  452 us (78%)
  local copies, waits for them, and re-layouts  66.6 us (12%)
  other arithmetic  19.4 us (3%)
  matrix products  14.2 us (2%)
  between operations  13.6 us (2%)
  starting transfers between devices  9.86 us (2%)
    all_to_all x1, waiting for transfers between devices, all_by_exchange(): pieces = lax.all_to_all(pieces, axis, split_axis=0, concat_axis=0)  187 us
    reduce_scatter x1, waiting for transfers between devices, on_device(): lax.psum_scatter(partial_value, 'ka', scatter_dimension=2, tiled=True)  184 us
    reduce_scatter x1, waiting for transfers between devices, on_device(): lax.psum_scatter(column_sums, 'band', scatter_dimension=1, tiled=True)  81.2 us
    convert_element_type x3, local copies, waits for them, and re-layouts, on_device(): product = weight[..., None] * rotated[None].astype(jnp.float32)  26.9 us
  transfers between devices with their start and end apart: 3, of which 3 were waited for; matrix products, arithmetic and copies ran while one was open for 1% of the time, Pallas kernels for 0%

profile of v1, /device:TPU:2, one launch (start us, length us, event | category | flops | bytes accessed | tf_op | source)
XLA Modules:
  0.0 575.9 jit_solution(12356700002823252195)
XLA Ops:
  6.5 0.0 copy-start
  6.5 5.4 stack.8
  11.9 0.0 copy-start.2
  11.9 0.0 copy-start.3
  11.9 0.0 copy-start.4
  11.9 0.0 copy-start.6
  11.9 0.0 copy-start.5
  12.0 9.8 %all-to-all-start = ((bf16[16,8,2,8,2048]{4,3,2,1,0:T(8,128)(2,1)}), bf16[16,8,2,8,2048]{4,3,2,1,0:T(8,128)(2,1)}, u32[]{:S(2)}, u32[]{:S(2)}) async-start(bf16[16,8,2,8,2048]{4,3,2,1,0:T(8,128)(2,1)} %stack.8), calls=%async_computation | async-start | bytes 16777216 | tf_op jit(solution)/shard_map/all_to_all | solution.py:17
  21.7 0.0 reduce-scatter.3.cloned.1.call-start
  21.8 0.0 copy-done.2
  21.8 0.6 gather_fusion.6
  22.5 0.0 copy-done.3
  22.5 0.6 gather_fusion.5
  23.1 0.0 copy-done.4
  23.1 0.6 gather_fusion.4
  23.8 0.1 iota_add_fusion
  23.8 0.1 add.71
  23.9 0.0 copy-done.6
  23.9 0.1 copy.18
  24.1 0.1 copy.19
  24.2 0.0 copy-done.5
  24.2 0.6 gather_fusion
  24.8 0.6 gather_fusion.1
  25.3 0.1 compare_convert_fusion
  25.4 0.1 broadcast_select_fusion.1
  25.5 0.1 broadcast_select_fusion
  25.6 0.1 fusion.7
  25.7 0.1 mul.115
  25.8 0.0 copy-done
  25.8 0.6 gather_fusion.2
  26.4 0.1 fusion.8
  26.4 187.1 %all-to-all-done = bf16[16,8,2,8,2048]{4,3,2,1,0:T(8,128)(2,1)} async-done(((bf16[16,8,2,8,2048]{4,3,2,1,0:T(8,128)(2,1)}), bf16[16,8,2,8,2048]{4,3,2,1,0:T(8,128)(2,1)}, u32[]{:S(2)}, u32[]{:S(2)}) %all-to-all-start) | async-done | bytes 8388640 | tf_op jit(solution)/shard_map/all_to_all | solution.py:17
  213.5 8.3 %copy.20 = bf16[16,8,2,8,2048]{4,3,2,0,1:T(8,128)(2,1)} copy(bf16[16,8,2,8,2048]{4,3,2,1,0:T(8,128)(2,1)} %all-to-all-done) | data formatting | bytes 16777216 | tf_op jit(solution)/shard_map/all_to_all | solution.py:17
  221.8 6.2 %gather_fusion.3 = bf16[4,32,8,2048]{3,2,1,0:T(8,128)(2,1)} fusion(bf16[8,32,8,2048]{3,2,1,0:T(8,128)(2,1)} %bitcast.36, s32[1024]{0:T(1024)S(1)} %pad_clamp_fusion.1), kind=kCustom, calls=%fused_computation.6 | custom fusion | bytes 8388624 | tf_op jit(solution)/shard_map/jit(_take)/gather | solution.py:46
  227.9 3.6 copy.28
  231.5 0.5 bitcast_select_fusion
  232.0 3.5 convert_bitcast_fusion
  235.5 6.4 %copy.24 = bf16[4,256,16,128]{3,1,0,2:T(8,128)(2,1)} copy(bf16[4,256,16,128]{1,3,2,0:T(8,128)(2,1)} %convert_bitcast_fusion) | data formatting | bytes 8388608 | tf_op jit(solution)/shard_map/convert_element_type | solution.py:28
  241.9 8.4 %copy.22 = f32[4,256,16,128]{3,2,1,0:T(8,128)} copy(bf16[4,256,16,128]{1,3,2,0:T(8,128)(2,1)} %convert_bitcast_fusion) | data formatting | bytes 12582912 | tf_op jit(solution)/shard_map/convert_element_type | solution.py:64
  250.3 9.3 %reshape.265 = f32[1,4,32,8,2048]{4,3,2,1,0:T(8,128)} reshape(f32[4,256,16,128]{3,2,1,0:T(8,128)} %copy.22) | data formatting | bytes 16777216 | tf_op jit(solution)/shard_map/convert_element_type | solution.py:64
  259.5 9.2 %reshape.264 = f32[1,1024,2048]{2,1,0:T(8,128)} reshape(f32[4,256,16,128]{3,2,1,0:T(8,128)} %copy.22) | data formatting | bytes 16777216 | tf_op jit(solution)/shard_map/convert_element_type | solution.py:64
  268.8 1.7 constant_dynamic-slice_fusion
  270.5 2.6 copy.25
  273.1 0.0 slice-start
  273.1 4.0 multiply_convert_fusion.1
  277.2 0.0 slice-start.1
  277.2 6.5 %subtract_convert_fusion = bf16[1,4,32,8,2048]{4,3,2,1,0:T(8,128)(2,1)} fusion(bf16[1,4,32,8,2048]{4,3,2,1,0:T(8,128)(2,1)S(1)} %multiply_convert_fusion.1, f32[1,4,32,8,2048]{4,3,2,1,0:T(8,128)} %reshape.265, f32[4,32,8]{2,1,0:T(8,128)S(1)} %fusion.7), kind=kLoop, calls=%fused_computation.8 | loop fusion | flops 8388608 | bytes 16781312 | tf_op jit(solution)/shard_map/convert_element_type | solution.py:67
  283.7 0.0 slice-done
  283.7 0.0 slice-done.1
  283.7 0.5 fusion
  284.2 7.4 %convert_reduce_fusion = bf16[1024,2048]{1,0:T(8,128)(2,1)} fusion(bf16[1,1,1024,2048]{3,2,1,0:T(8,128)(2,1)} %bitcast.37, bf16[1,1,1024,2048]{3,2,1,0:T(8,128)(2,1)S(1)} %fusion), kind=kLoop, calls=%fused_computation.7 | loop fusion | flops 18874368 | bytes 12582912 | tf_op jit(solution)/shard_map/rg,sfrh->fgh/reduce_sum | solution.py:78
  291.6 10.7 %convolution_bitcast_fusion = f32[1,1024,2048]{1,2,0:T(8,128)} fusion(bf16[1024,2048]{1,0:T(8,128)(2,1)} %convert_reduce_fusion, bf16[1024,1024]{0,1:T(8,128)(2,1)} %bitcast.41), kind=kOutput, calls=%fused_computation.11 | convolution fusion | flops 4294967296 | bytes 14680064 | tf_op jit(solution)/shard_map/rg,sfrh->fgh/dot_general | solution.py:78
  302.3 0.0 copy-start.1
  302.3 0.0 reduce-scatter.3.cloned.1.call-update
  302.3 0.0 reduce-scatter.5.cloned.1.call-start
  302.3 184.0 %reduce-scatter.3.cloned.1.call-done = f32[1,1024,128]{1,2,0:T(8,128)} async-done(((f32[1,1024,2048]{1,2,0:T(8,128)}), f32[1,1024,128]{1,2,0:T(8,128)}) %reduce-scatter.3.cloned.1.call-update) | async-done | bytes 524304 | tf_op jit(solution)/shard_map/reduce_scatter | solution.py:81
  486.4 0.0 reduce-scatter.5.cloned.1.call-update
  486.4 81.2 %reduce-scatter.5.cloned.1.call-done = f32[1,128,128]{1,2,0:T(8,128)} async-done(((f32[1,1024,128]{1,2,0:T(8,128)}), f32[1,128,128]{1,2,0:T(8,128)}) %reduce-scatter.5.cloned.1.call-update) | async-done | bytes 65552 | tf_op jit(solution)/shard_map/reduce_scatter | solution.py:82
  567.5 1.6 copy.26
  569.1 0.0 copy-done.1
  (10 shorter events, 0.1 us)
Async XLA Ops:
  6.5 19.2 %copy-start = (s32[48,2048]{1,0:T(8,128)S(1)}, s32[48,2048]{1,0:T(8,128)}, u32[]{:S(2)}) copy-start(s32[48,2048]{1,0:T(8,128)} %param.14) | copy-start | bytes 1179652
  11.9 9.9 %copy-start.2 = (s32[64]{0:T(128)S(1)}, s32[64]{0:T(128)}, u32[]{:S(2)}) copy-start(s32[64]{0:T(128)} %param.13) | copy-start | bytes 772
  11.9 10.5 %copy-start.3 = (s32[64]{0:T(128)S(1)}, s32[64]{0:T(128)}, u32[]{:S(2)}) copy-start(s32[64]{0:T(128)} %param.15) | copy-start | bytes 772
  11.9 11.2 %copy-start.4 = (s32[64]{0:T(128)S(1)}, s32[64]{0:T(128)}, u32[]{:S(2)}) copy-start(s32[64]{0:T(128)} %param.12) | copy-start | bytes 772
  11.9 12.0 %copy-start.6 = (f32[8,256]{1,0:T(8,128)S(1)}, f32[8,256]{1,0:T(8,128)}, u32[]{:S(2)}) copy-start(f32[8,256]{1,0:T(8,128)} %param.11) | copy-start | bytes 24580
  11.9 12.3 %copy-start.5 = (f32[8,8]{1,0:T(8,128)S(1)}, f32[8,8]{1,0:T(8,128)}, u32[]{:S(2)}) copy-start(f32[8,8]{1,0:T(8,128)} %param.10) | copy-start | bytes 772
  12.0 201.5 %all-to-all-start = ((bf16[16,8,2,8,2048]{4,3,2,1,0:T(8,128)(2,1)}), bf16[16,8,2,8,2048]{4,3,2,1,0:T(8,128)(2,1)}, u32[]{:S(2)}, u32[]{:S(2)}) async-start(bf16[16,8,2,8,2048]{4,3,2,1,0:T(8,128)(2,1)} %stack.8), calls=%async_computation | async-start | bytes 16777216 | tf_op jit(solution)/shard_map/all_to_all | solution.py:17
  21.7 464.6 %reduce-scatter.3.cloned.1.call-start = ((), (), s32[]{:S(2)}) async-start(), calls=%async_computation.3 | async-start | bytes 8912896 | tf_op jit(solution)/shard_map/reduce_scatter | solution.py:81
  273.1 10.5 %slice-start = ((s8[8388608]{0:T(1024)(128)(4,1)}), s8[4194304]{0:T(1024)(128)(4,1)S(1)}, s32[]{:S(2)}) async-start(s8[8388608]{0:T(1024)(128)(4,1)} %bitcast.34), calls=%async_computation.5 | async-start | bytes 8388608
  277.2 6.5 %slice-start.1 = ((s8[8388608]{0:T(1024)(128)(4,1)}), s8[4194304]{0:T(1024)(128)(4,1)S(1)}, s32[]{:S(2)}) async-start(s8[8388608]{0:T(1024)(128)(4,1)} %bitcast.34), calls=%async_computation.6 | async-start | bytes 8388608
  302.3 266.8 %copy-start.1 = (s32[48,2048]{1,0:T(8,128)S(1)}, s32[48,2048]{1,0:T(8,128)}, u32[]{:S(2)}) copy-start(s32[48,2048]{1,0:T(8,128)} %param.14) | copy-start | bytes 1179652
  302.3 265.2 %reduce-scatter.5.cloned.1.call-start = ((), (), s32[]{:S(2)}) async-start(), calls=%async_computation.4 | async-start | bytes 589824 | tf_op jit(solution)/shard_map/reduce_scatter | solution.py:82
Sparse Core Ops, SparseCore 0:
  302.4 183.8 reduce-scatter.2
  490.2 77.2 reduce-scatter.4
